TPU v7x, 128 devices: a whole 4x4x4 slice. The times are simulated.
128 devices in a mesh: row: 16 (over x, z), col: 8 (over y, core).
Axes of the slice: x: 4, y: 4, z: 4, core: 2. Of those that a mesh axis runs over, the one named last changes fastest.
Arguments:
- a_vals: float32 [16, 8, 448, 4096], P('row', 'col'), may hold values from -0.1875 to 0.1875
- a_row: int32 [16, 8, 448], P('row', 'col'), may hold values from 0 to 63
- a_col: int32 [16, 8, 448], P('row', 'col'), may hold values from 0 to 127
- a_slot: int32 [16, 8, 3, 448], P('row', 'col'), may hold values from 0 to 5
- a_count: int32 [16, 8], P('row', 'col'), may hold values from 1 to 448, as said below
- p_vals: float32 [1024, 3, 4096], P(('row', 'col')), may hold values from -0.75 to 0.75
- p_owner: int32 [1024, 3], P(('row', 'col')), may hold values from 0 to 15, all different within a row; in each aligned block of 8 rows (0 to 7, 8 to 15, ...) at most 2 rows name the same one
- p_sub: int32 [1024, 3], P(('row', 'col')), may hold values from 0 to 7
- ap_cslot: int32 [1024, 3, 6], P(('row', 'col')), may hold values from 0 to 26
Outputs:
- coarse: float32 [128, 27, 4096], P(('row', 'col'))
Inputs may be any that keep to these rules, and one draw needn't show every extreme that they name: `a_count`: at least one device holds exactly 448 listed blocks. `p_owner`: the 3 entries of a fine block row differ; among the rows of one device each row group is named at most 2 times.
All inputs are finite; a program needn't handle non-finite values.
Results may differ from a plain program's by a relative error of at most 0.0001.
Values sent between devices are 32-bit elements; how exact they have to be, the bound alone decides.
No kernel may reach another device: no remote copies, remote signals or barrier semaphores. Data moves between devices by JAX's collectives and lax.ppermute only.
A program may use at most 128 MiB of HBM per device.

v0:
```python
import jax
import jax.numpy as jnp
from jax import lax
from jax.sharding import PartitionSpec as P

BLOCK = 64
CPD = 1
TAP = 6
TC = 27
highest = lax.Precision.HIGHEST
tile_batch = 16


def on_device(a_vals, a_row, a_col, a_slot, a_count, p_vals, p_owner, p_sub, ap_cslot):
    row_devices = lax.axis_size("row")
    col_devices = lax.axis_size("col")
    capacity = a_vals.shape[2]
    rows_dev = p_vals.shape[0]
    branches = p_vals.shape[1]
    tile_len = p_vals.shape[2]
    group_rows = rows_dev * col_devices
    group_coarse = CPD * col_devices
    per_peer = max(2, 3 * rows_dev * branches // (2 * row_devices))
    matrix_tiles = a_vals.reshape(capacity, BLOCK, BLOCK)
    tile_rows = a_row.reshape(capacity)
    tile_cols = a_col.reshape(capacity)
    tile_slots = a_slot.reshape(branches, capacity)
    tile_count = a_count.reshape(())
    panel = lax.all_gather(p_vals, "row", axis=0, tiled=True)
    panel_tiles = panel.reshape(rows_dev * row_devices, branches, BLOCK, BLOCK)

    def add_batch(batch_index, partial_value):
        first_tile = batch_index * tile_batch
        block_tiles = lax.dynamic_slice_in_dim(matrix_tiles, first_tile, tile_batch, 0)
        block_rows = lax.dynamic_slice_in_dim(tile_rows, first_tile, tile_batch, 0)
        block_cols = lax.dynamic_slice_in_dim(tile_cols, first_tile, tile_batch, 0)
        block_slots = lax.dynamic_slice_in_dim(tile_slots, first_tile, tile_batch, 1)
        right_tiles = jnp.take(panel_tiles, block_cols, axis=0)
        products = jnp.einsum("tij,tsjk->tsik", block_tiles, right_tiles, precision=highest)
        is_live = first_tile + jnp.arange(tile_batch, dtype=jnp.int32) < tile_count
        products = jnp.where(is_live[:, None, None, None], products, 0.0)
        target = block_rows[:, None] * TAP + block_slots.T
        return partial_value.at[target.reshape(-1)].add(
            products.reshape(tile_batch * branches, tile_len)
        )

    batches = (tile_count + tile_batch - 1) // tile_batch
    partial_value = lax.fori_loop(
        0, batches, add_batch, jnp.zeros((group_rows * TAP, tile_len), jnp.float32)
    )
    ap_rows = lax.psum_scatter(
        partial_value.reshape(group_rows, TAP, tile_len), "col", scatter_dimension=0, tiled=True
    )
    item_count = rows_dev * branches
    owners = p_owner.reshape(item_count)
    serial = jnp.arange(item_count, dtype=jnp.int32)
    earlier = (owners[:, None] == owners[None, :]) & (serial[None, :] < serial[:, None])
    placed = owners * per_peer + jnp.sum(earlier.astype(jnp.int32), axis=1)
    slots_total = row_devices * per_peer
    metadata = jnp.concatenate(
        [p_sub.reshape(item_count, 1), ap_cslot.reshape(item_count, TAP)], axis=1
    ).astype(jnp.float32)
    meta_send = jnp.zeros((slots_total, TAP + 1), jnp.float32).at[placed].set(metadata)
    ap_items = jnp.broadcast_to(ap_rows[:, None], (rows_dev, branches, TAP, tile_len)).reshape(
        item_count, TAP, tile_len
    )
    packed = jnp.concatenate([p_vals.reshape(item_count, 1, tile_len), ap_items], axis=1)
    outgoing = jnp.zeros((slots_total, TAP + 1, tile_len), jnp.float32).at[placed].set(packed)
    incoming, meta_in = (
        lax.all_to_all(outgoing, "row", split_axis=0, concat_axis=0, tiled=True),
        lax.all_to_all(meta_send, "row", split_axis=0, concat_axis=0, tiled=True),
    )
    left_in = incoming[:, 0].reshape(slots_total, BLOCK, BLOCK)
    right_in = incoming[:, 1:].reshape(slots_total, TAP, BLOCK, BLOCK)
    arrived = jnp.einsum("ejk,eqjl->eqkl", left_in, right_in, precision=highest).reshape(
        slots_total, TAP, tile_len
    )
    arrived_index = meta_in.astype(jnp.int32)
    target = arrived_index[:, :1] * TC + arrived_index[:, 1:]
    coarse_part = (
        jnp.zeros((group_coarse * TC, tile_len), jnp.float32)
        .at[target.reshape(-1)]
        .add(arrived.reshape(slots_total * TAP, tile_len))
    )
    coarse = lax.psum_scatter(
        coarse_part.reshape(group_coarse, TC, tile_len), "col", scatter_dimension=0, tiled=True
    )
    return coarse


def solution(mesh):
    placed = (
        P("row", "col", None, None),
        P("row", "col", None),
        P("row", "col", None),
        P("row", "col", None, None),
        P("row", "col"),
        P(("row", "col"), None, None),
        P(("row", "col"), None),
        P(("row", "col"), None),
        P(("row", "col"), None, None),
    )
    return jax.shard_map(
        on_device,
        mesh=mesh,
        in_specs=placed,
        out_specs=P(("row", "col"), None, None),
        check_vma=False,
    )
```

profile of v0, /device:TPU:0, one launch (start us, length us, event | category | flops | bytes accessed | tf_op | source)
XLA Modules:
  0.0 882.7 jit_solution(11410659418948693144)
XLA Ops:
  8.0 9.0 %copy.84 = f32[1,1,448,4096]{2,3,1,0:T(8,128)} copy(f32[1,1,448,4096]{3,2,1,0:T(8,128)} %param.11) | data formatting | bytes 14680064 | tf_op args[0]
  17.0 11.9 %copy.86 = f32[448,64,64]{2,1,0:T(8,128)} copy(f32[448,64,64]{0,2,1:T(8,128)} %bitcast.49) | data formatting | bytes 14680064 | tf_op jit(solution)/shard_map/while | solution.py:48
  29.0 44.5 %all-gather.2.cloned.1.call-done = f32[128,3,4096]{2,0,1:T(8,128)} async-done(((f32[8,3,4096]{2,0,1:T(8,128)}), f32[128,3,4096]{2,0,1:T(8,128)}) %all-gather.2.cloned.1.call-update) | async-done | bytes 6291472 | tf_op jit(solution)/shard_map/all_gather | solution.py:29
  73.5 6.6 copy.83
  80.1 12.7 %copy.85 = f32[128,3,64,64]{3,2,1,0:T(8,128)} copy(f32[128,3,64,64]{0,3,2,1:T(8,128)} %bitcast.50) | data formatting | bytes 12582912 | tf_op jit(solution)/shard_map/while | solution.py:48
  96.2 38.7 %while.10 = (s32[]{:T(128)}, f32[384,4096]{1,0:T(8,128)}, s32[]{:T(128)}, s32[448]{0:T(512)}, s32[3,448]{0,1:T(8,128)S(1)}, /*index=5*/s32[]{:T(128)}, s32[448]{...) while((s32[]{:T(128)}, f32[384,4096]{1,0:T(8,128)}, ...), condition=%wide.region_4.5_spmd, body=%wide.region_2.4_spmd.sunk | while | flops 151586128 | bytes 9181187 | solution.py:48
  97.6 5.2 gather_fusion
  108.6 6.9 scatter_fusion
  116.9 5.2 gather_fusion
  122.2 3.9 select_bitcast_fusion.2
  128.0 6.9 scatter_fusion
  134.9 7.5 reshape.161
  145.3 508.0 %all-to-all-start = ((f32[16,2,7]{2,1,0:T(2,128)}), f32[16,2,7]{2,1,0:T(2,128)S(1)}, u32[]{:S(2)}, u32[]{:S(2)}) async-start(f32[16,2,7]{2,1,0:T(2,128)} %bitcast.7), calls=%async_computation | async-start | bytes 32768 | tf_op jit(solution)/shard_map/all_to_all | solution.py:71
  653.8 43.9 %reduce-scatter.3.cloned.1.call-done = f32[8,6,4096]{2,1,0:T(8,128)} async-done(((f32[64,6,4096]{2,1,0:T(8,128)}), f32[8,6,4096]{2,1,0:T(8,128)}) %reduce-scatter.3.cloned.1.call-update) | async-done | bytes 786448 | tf_op jit(solution)/shard_map/reduce_scatter | solution.py:51
  708.7 6.6 scatter_fusion.1
  715.3 7.0 all-to-all-start.1
  722.6 56.7 %all-to-all-done.1 = f32[32,7,4096]{2,1,0:T(8,128)} async-done(((f32[32,7,4096]{2,1,0:T(8,128)}), f32[32,7,4096]{2,1,0:T(8,128)}, u32[]{:S(2)}, u32[]{:S(2)}) %all-to-all-start.1) | async-done | bytes 3670048 | tf_op jit(solution)/shard_map/all_to_all | solution.py:70
  779.3 5.1 slice.20
  784.4 6.8 reshape.208
  795.2 13.3 %convolution_bitcast_fusion = f32[32,6,64,64]{2,3,1,0:T(8,128)} fusion(f32[32,6,64,64]{3,2,1,0:T(8,128)} %reshape.208, f32[32,64,64,1]{2,1,0,3:T(8,128)S(1)} %reshape.207), kind=kOutput, calls=%fused_computation.23 | convolution fusion | flops 603979776 | bytes 6815744 | tf_op jit(solution)/shard_map/ejk,eqjl->eqkl/dot_general | solution.py:75
  808.5 6.6 copy.91
  815.1 5.9 reshape.201
  821.0 6.7 scatter_custom_fusion.3
  830.2 43.8 %reduce-scatter.5.cloned.1.call-done = f32[1,27,4096]{2,1,0:T(8,128)} async-done(((f32[8,27,4096]{2,1,0:T(8,128)}), f32[1,27,4096]{2,1,0:T(8,128)}) %reduce-scatter.5.cloned.1.call-update) | async-done | bytes 442384 | tf_op jit(solution)/shard_map/reduce_scatter | solution.py:85
  (71 shorter events, 38.0 us)
Async XLA Ops:
  6.5 66.9 %all-gather.2.cloned.1.call-start = ((), (), s32[]{:S(2)}) async-start(), calls=%async_computation.4 | async-start | bytes 6684672 | tf_op jit(solution)/shard_map/all_gather | solution.py:29
  7.3 690.4 %reduce-scatter.3.cloned.1.call-start = ((), (), s32[]{:S(2)}) async-start(), calls=%async_computation.5 | async-start | bytes 9437184 | tf_op jit(solution)/shard_map/reduce_scatter | solution.py:51
  17.0 11.9 %copy-start.3 = (s32[1,1,3,448]{3,1,2,0:T(1,128)S(1)}, s32[1,1,3,448]{3,1,2,0:T(1,128)}, u32[]{:S(2)}) copy-start(s32[1,1,3,448]{3,1,2,0:T(1,128)} %param.14) | copy-start | bytes 16132
  142.4 0.7 copy-start.2
  142.4 1.0 copy-start.1
  142.4 1.2 copy-start.4
  142.4 510.9 %copy-start = (f32[8,3,4096]{2,0,1:T(8,128)S(1)}, f32[8,3,4096]{2,0,1:T(8,128)}, u32[]{:S(2)}) copy-start(f32[8,3,4096]{2,0,1:T(8,128)} %param.16) | copy-start | bytes 1179652
  144.1 1.2 copy-start.5
  145.3 570.0 %all-to-all-start = ((f32[16,2,7]{2,1,0:T(2,128)}), f32[16,2,7]{2,1,0:T(2,128)S(1)}, u32[]{:S(2)}, u32[]{:S(2)}) async-start(f32[16,2,7]{2,1,0:T(2,128)} %bitcast.7), calls=%async_computation | async-start | bytes 32768 | tf_op jit(solution)/shard_map/all_to_all | solution.py:71
  706.2 2.4 copy-start.6
  715.3 64.1 %all-to-all-start.1 = ((f32[32,7,4096]{2,1,0:T(8,128)}), f32[32,7,4096]{2,1,0:T(8,128)}, u32[]{:S(2)}, u32[]{:S(2)}) async-start(f32[32,7,4096]{2,1,0:T(8,128)} %scatter_fusion.1), calls=%async_computation.2 | async-start | bytes 8388608 | tf_op jit(solution)/shard_map/all_to_all | solution.py:70
  722.3 151.7 %reduce-scatter.5.cloned.1.call-start = ((), (), s32[]{:S(2)}) async-start(), calls=%async_computation.6 | async-start | bytes 4718592 | tf_op jit(solution)/shard_map/reduce_scatter | solution.py:85
Sparse Core Ops, SparseCore 0:
  9.5 63.8 all-gather.1
  142.6 555.0 reduce-scatter.2
  830.3 43.5 reduce-scatter.4
where the time goes:
time: 889 us; the launch traced here: 883 us
  starting transfers between devices  515 us (58%)
  waiting for transfers between devices  190 us (21%)
  local copies, waits for them, and re-layouts  116 us (13%)
  other arithmetic  27.3 us (3%)
  matrix products  21 us (2%)
  between operations  14 us (2%)
    all_to_all x1, starting transfers between devices, on_device(): lax.all_to_all(meta_send, 'row', split_axis=0, concat_axis=0, tiled=True)  508 us
    all_to_all x1, waiting for transfers between devices, on_device(): lax.all_to_all(outgoing, 'row', split_axis=0, concat_axis=0, tiled=True)  56.7 us
    all_gather x1, waiting for transfers between devices, on_device(): panel = lax.all_gather(p_vals, 'row', axis=0, tiled=True)  44.5 us
    reduce_scatter x1, waiting for transfers between devices, on_device(): lax.psum_scatter(partial_value.reshape(group_rows, TAP, tile_len), 'col',...  43.9 us
    reduce_scatter x1, waiting for transfers between devices, on_device(): lax.psum_scatter(coarse_part.reshape(group_coarse, TC, tile_len), 'col',...  43.8 us
    while x2, local copies, waits for them, and re-layouts, on_device(): lax.fori_loop(0, batches, add_batch, jnp.zeros((group_rows * TAP, tile_le...  24.6 us
  transfers between devices with their start and end apart: 5, of which 4 were waited for; matrix products, arithmetic and copies ran while one was open for 5% of the time, Pallas kernels for 0%

commit v1 on v0

--- a/solution.py
+++ b/solution.py
@@ -26,7 +26,14 @@
     tile_cols = a_col.reshape(capacity)
     tile_slots = a_slot.reshape(branches, capacity)
     tile_count = a_count.reshape(())
-    panel = lax.all_gather(p_vals, "row", axis=0, tiled=True)
+    amount_of = lax.axis_size("row")
+    panel = lax.all_to_all(
+        jnp.tile(p_vals, [amount_of if i0 == 0 else 1 for i0 in range(p_vals.ndim)]),
+        "row",
+        split_axis=0,
+        concat_axis=0,
+        tiled=True,
+    )
     panel_tiles = panel.reshape(rows_dev * row_devices, branches, BLOCK, BLOCK)
 
     def add_batch(batch_index, partial_value):

time: 889 us -> 995 us (1.12)
  waiting for transfers between devices: 190 us -> 270 us
  local copies, waits for them, and re-layouts: 116 us -> 128 us
  starting transfers between devices: 515 us -> 527 us
    all_to_all x0 -> x1, waiting for transfers between devices: none -> 126 us  [on_device(): lax.all_to_all(jnp.tile(p_vals, [amount_of if i0 == 0 else 1 for i0 in ra...]
    all_gather x1 -> x0, waiting for transfers between devices: 44.5 us -> none  [on_device(): panel = lax.all_gather(p_vals, 'row', axis=0, tiled=True)]
  transfers between devices with their start and end apart: 5 -> 5, of which waited for: 4 -> 4; matrix products, arithmetic and copies ran while one was open for 5% -> 4% of each run, Pallas kernels for 0% -> 0%
where the time goes in v1:
time: 995 us; the launch traced here: 988 us
  starting transfers between devices  527 us (53%)
  waiting for transfers between devices  270 us (27%)
  local copies, waits for them, and re-layouts  128 us (13%)
  other arithmetic  27.3 us (3%)
  matrix products  21 us (2%)
  between operations  14.3 us (1%)
    all_to_all x1, starting transfers between devices, on_device(): lax.all_to_all(meta_send, 'row', split_axis=0, concat_axis=0, tiled=True)  512 us
    all_to_all x1, waiting for transfers between devices, on_device(): lax.all_to_all(jnp.tile(p_vals, [amount_of if i0 == 0 else 1 for i0 in ra...  126 us
    all_to_all x1, waiting for transfers between devices, on_device(): lax.all_to_all(outgoing, 'row', split_axis=0, concat_axis=0, tiled=True)  56.7 us
    reduce_scatter x1, waiting for transfers between devices, on_device(): lax.psum_scatter(coarse_part.reshape(group_coarse, TC, tile_len), 'col',...  44 us
    reduce_scatter x1, waiting for transfers between devices, on_device(): lax.psum_scatter(partial_value.reshape(group_rows, TAP, tile_len), 'col',...  43.8 us
    while x2, local copies, waits for them, and re-layouts, on_device(): lax.fori_loop(0, batches, add_batch, jnp.zeros((group_rows * TAP, tile_le...  24.6 us
  transfers between devices with their start and end apart: 5, of which 4 were waited for; matrix products, arithmetic and copies ran while one was open for 4% of the time, Pallas kernels for 0%

profile of v1, /device:TPU:0, one launch (start us, length us, event | category | flops | bytes accessed | tf_op | source)
XLA Modules:
  0.0 988.1 jit_solution(5635718491444892311)
XLA Ops:
  8.3 7.7 copy.84
  15.9 8.0 all-to-all-start.1
  24.7 9.0 copy.86
  33.7 11.8 %copy.88 = f32[448,64,64]{2,1,0:T(8,128)} copy(f32[448,64,64]{0,2,1:T(8,128)} %bitcast.51) | data formatting | bytes 14680064 | tf_op jit(solution)/shard_map/while | solution.py:55
  45.7 125.9 %all-to-all-done.1 = f32[128,3,4096]{2,1,0:T(4,128)} async-done(((f32[128,3,4096]{2,1,0:T(4,128)}), f32[128,3,4096]{2,1,0:T(4,128)}, u32[]{:S(2)}, u32[]{:S(2)}) %all-to-all-start.1) | async-done | bytes 6291488 | tf_op jit(solution)/shard_map/all_to_all | solution.py:30
  171.5 9.1 copy.85
  180.6 12.7 %copy.87 = f32[128,3,64,64]{3,2,1,0:T(8,128)} copy(f32[128,3,64,64]{0,3,2,1:T(8,128)} %bitcast.52) | data formatting | bytes 12582912 | tf_op jit(solution)/shard_map/while | solution.py:55
  196.7 38.7 %while.10 = (s32[]{:T(128)}, f32[384,4096]{1,0:T(8,128)}, s32[]{:T(128)}, s32[448]{0:T(512)}, s32[3,448]{0,1:T(8,128)S(1)}, /*index=5*/s32[]{:T(128)}, s32[448]{...) while((s32[]{:T(128)}, f32[384,4096]{1,0:T(8,128)}, ...), condition=%wide.region_4.5_spmd, body=%wide.region_2.4_spmd.sunk | while | flops 151586128 | bytes 9181187 | solution.py:55
  198.1 5.2 gather_fusion
  209.2 6.9 scatter_fusion
  217.5 5.2 gather_fusion
  228.5 6.9 scatter_fusion
  235.4 7.5 reshape.165
  245.9 512.3 %all-to-all-start = ((f32[16,2,7]{2,1,0:T(2,128)}), f32[16,2,7]{2,1,0:T(2,128)S(1)}, u32[]{:S(2)}, u32[]{:S(2)}) async-start(f32[16,2,7]{2,1,0:T(2,128)} %bitcast.7), calls=%async_computation | async-start | bytes 32768 | tf_op jit(solution)/shard_map/all_to_all | solution.py:78
  758.7 43.8 %reduce-scatter.3.cloned.1.call-done = f32[8,6,4096]{2,1,0:T(8,128)} async-done(((f32[64,6,4096]{2,1,0:T(8,128)}), f32[8,6,4096]{2,1,0:T(8,128)}) %reduce-scatter.3.cloned.1.call-update) | async-done | bytes 786448 | tf_op jit(solution)/shard_map/reduce_scatter | solution.py:58
  813.5 6.6 scatter_fusion.1
  820.1 7.0 all-to-all-start.2
  827.5 56.7 %all-to-all-done.2 = f32[32,7,4096]{2,1,0:T(8,128)} async-done(((f32[32,7,4096]{2,1,0:T(8,128)}), f32[32,7,4096]{2,1,0:T(8,128)}, u32[]{:S(2)}, u32[]{:S(2)}) %all-to-all-start.2) | async-done | bytes 3670048 | tf_op jit(solution)/shard_map/all_to_all | solution.py:77
  889.3 6.8 reshape.212
  900.1 13.3 %convolution_bitcast_fusion = f32[32,6,64,64]{2,3,1,0:T(8,128)} fusion(f32[32,6,64,64]{3,2,1,0:T(8,128)} %reshape.212, f32[32,64,64,1]{2,1,0,3:T(8,128)S(1)} %reshape.211), kind=kOutput, calls=%fused_computation.24 | convolution fusion | flops 603979776 | bytes 6815744 | tf_op jit(solution)/shard_map/ejk,eqjl->eqkl/dot_general | solution.py:82
  913.3 6.6 copy.93
  919.9 5.9 reshape.205
  925.8 6.7 scatter_custom_fusion.3
  935.0 44.0 %reduce-scatter.5.cloned.1.call-done = f32[1,27,4096]{2,1,0:T(8,128)} async-done(((f32[8,27,4096]{2,1,0:T(8,128)}), f32[1,27,4096]{2,1,0:T(8,128)}) %reduce-scatter.5.cloned.1.call-update) | async-done | bytes 442384 | tf_op jit(solution)/shard_map/reduce_scatter | solution.py:92
  (72 shorter events, 48.0 us)
Async XLA Ops:
  15.9 155.6 %all-to-all-start.1 = ((f32[128,3,4096]{2,1,0:T(4,128)}), f32[128,3,4096]{2,1,0:T(4,128)}, u32[]{:S(2)}, u32[]{:S(2)}) async-start(f32[128,3,4096]{2,1,0:T(4,128)} %copy.84), calls=%async_computation.1 | async-start | bytes 16777216 | tf_op jit(solution)/shard_map/all_to_all | solution.py:30
  24.0 778.5 %reduce-scatter.3.cloned.1.call-start = ((), (), s32[]{:S(2)}) async-start(), calls=%async_computation.5 | async-start | bytes 9437184 | tf_op jit(solution)/shard_map/reduce_scatter | solution.py:58
  33.7 11.8 %copy-start.3 = (s32[1,1,3,448]{3,1,2,0:T(1,128)S(1)}, s32[1,1,3,448]{3,1,2,0:T(1,128)}, u32[]{:S(2)}) copy-start(s32[1,1,3,448]{3,1,2,0:T(1,128)} %param.14) | copy-start | bytes 16132
  243.0 0.7 copy-start.2
  243.0 1.0 copy-start.1
  243.0 1.2 copy-start.4
  243.0 515.3 %copy-start = (f32[8,3,4096]{2,0,1:T(8,128)S(1)}, f32[8,3,4096]{2,0,1:T(8,128)}, u32[]{:S(2)}) copy-start(f32[8,3,4096]{2,0,1:T(8,128)} %param.16) | copy-start | bytes 1179652
  244.6 1.2 copy-start.5
  245.9 574.2 %all-to-all-start = ((f32[16,2,7]{2,1,0:T(2,128)}), f32[16,2,7]{2,1,0:T(2,128)S(1)}, u32[]{:S(2)}, u32[]{:S(2)}) async-start(f32[16,2,7]{2,1,0:T(2,128)} %bitcast.7), calls=%async_computation | async-start | bytes 32768 | tf_op jit(solution)/shard_map/all_to_all | solution.py:78
  811.0 2.4 copy-start.6
  820.1 64.1 %all-to-all-start.2 = ((f32[32,7,4096]{2,1,0:T(8,128)}), f32[32,7,4096]{2,1,0:T(8,128)}, u32[]{:S(2)}, u32[]{:S(2)}) async-start(f32[32,7,4096]{2,1,0:T(8,128)} %scatter_fusion.1), calls=%async_computation.3 | async-start | bytes 8388608 | tf_op jit(solution)/shard_map/all_to_all | solution.py:77
  827.1 151.9 %reduce-scatter.5.cloned.1.call-start = ((), (), s32[]{:S(2)}) async-start(), calls=%async_computation.6 | async-start | bytes 4718592 | tf_op jit(solution)/shard_map/reduce_scatter | solution.py:92
Sparse Core Ops, SparseCore 0:
  243.1 559.3 reduce-scatter.2
  935.1 43.8 reduce-scatter.4
